TPU v7x, 256 devices: a whole 4x4x8 slice. The times are simulated.
256 devices in a mesh: segment: 4 (over z_lo), expert: 64 (over x, y, z_hi, core).
Axes of the slice: x: 4, y: 4, z: 8 (z_hi: 2, z_lo: 4; z = z_hi * 4 + z_lo), core: 2. Of those that a mesh axis runs over, the one named last changes fastest.
Arguments:
- forward_input: bfloat16 [4, 512, 7168], P('segment', 'expert'), may hold values from -6 to 6
- forward_routes: int32 [4, 512, 8], P('segment', 'expert'), may hold values from 0 to 15, all different within a row; in each aligned block of 8 rows (0 to 7, 8 to 15, ..., all dimensions but the last counted through in order) at most 8 rows name the same one
- forward_gates: float32 [4, 512, 8], P('segment', 'expert'), may hold values from 0.05 to 0.8
- gate_matrix: bfloat16 [4, 64, 7168, 256], P('segment', 'expert'), may hold values from -0.0625 to 0.0625
- up_matrix: bfloat16 [4, 64, 7168, 256], P('segment', 'expert'), may hold values from -0.0625 to 0.0625
- down_matrix: bfloat16 [4, 64, 256, 7168], P('segment', 'expert'), may hold values from -0.1875 to 0.1875
Outputs:
- next_input: bfloat16 [4, 512, 7168], P('segment', 'expert')
Inputs may be any that keep to these rules, and one draw needn't show every extreme that they name: `forward_routes`: each token names 8 different experts. Among the 8 tokens of one index of expert, no expert is named by more than 8 of them, and in every draw some expert is named by exactly 8 tokens of some index.
All inputs are finite; a program needn't handle non-finite values.
Results may differ from a plain program's by a relative error of at most 0.0065.
Values may be sent and summed in bfloat16 or wider, within the bound.
No kernel may reach another device: no remote copies, remote signals or barrier semaphores. Data moves between devices by JAX's collectives and lax.ppermute only.
A program may use at most 128 MiB of HBM per device.

v0:
```python
import jax
import jax.numpy as jnp
from jax import lax
from jax.sharding import PartitionSpec as P

FH = 1024


def passed_along(value, axis, steps):
    count = lax.axis_size(axis)
    pairs = [(source, (source + steps) % count) for source in range(count)]
    return lax.ppermute(value, axis, pairs)


def slot_table(routes, experts, capacity):
    route_count = routes.shape[0] * routes.shape[1]
    flat_routes = routes.reshape(-1)
    onehot = (flat_routes[:, None] == jnp.arange(experts, dtype=jnp.int32)[None, :]).astype(
        jnp.int32
    )
    before = jnp.cumsum(onehot, axis=0) - onehot
    ranking = jnp.sum(before * onehot, axis=1)
    position = flat_routes * capacity + ranking
    source_row = (
        jnp.zeros((experts * capacity,), jnp.int32)
        .at[position]
        .set(jnp.arange(route_count, dtype=jnp.int32))
    )
    filled = jnp.zeros((experts * capacity,), jnp.int32).at[position].set(1)
    return (position, source_row, filled)


def expert_forward(row_block, gate_mat, upper_mat, down_mat):
    gate_act = jnp.dot(row_block, gate_mat, preferred_element_type=jnp.float32)
    upper_act = jnp.dot(row_block, upper_mat, preferred_element_type=jnp.float32)
    hidden = (jax.nn.silu(gate_act) * upper_act).astype(jnp.bfloat16)
    return jnp.dot(hidden, down_mat, preferred_element_type=jnp.float32).astype(jnp.bfloat16)


def local(forward_input, forward_routes, forward_gates, gate_matrix, up_matrix, down_matrix):
    devices = lax.axis_size("expert")
    hidden_slice = gate_matrix.shape[3]
    split = FH // hidden_slice
    groups = devices // split
    tokens = forward_input[0]
    token_count = forward_routes.shape[1]
    top_count = forward_routes.shape[2]
    model_width = tokens.shape[1]
    needed = (token_count * top_count + groups - 1) // groups + token_count * top_count // (
        4 * groups
    )
    capacity = min(token_count - token_count % split, split * ((needed + split - 1) // split))
    gate_mat = gate_matrix[0, 0]
    upper_mat = up_matrix[0, 0]
    down_mat = down_matrix[0, 0]
    zero_value = jnp.zeros((), jnp.bfloat16)
    place, source, filled = slot_table(forward_routes[0], groups, capacity)
    packed = jnp.where(filled[:, None] > 0, tokens[source // top_count], zero_value)
    packed = packed.reshape(groups, capacity, model_width)
    copies = jnp.broadcast_to(packed[None], (split, groups, capacity, model_width)).reshape(
        devices, capacity, model_width
    )
    received = lax.all_to_all(copies, "expert", split_axis=0, concat_axis=0, tiled=True)
    result = expert_forward(received.reshape(-1, model_width), gate_mat, upper_mat, down_mat)
    returned = lax.all_to_all(
        result.reshape(devices, capacity, model_width),
        "expert",
        split_axis=0,
        concat_axis=0,
        tiled=True,
    )
    added = jnp.sum(
        returned.astype(jnp.float32).reshape(split, groups, capacity, model_width), axis=0
    )
    summed = added.astype(jnp.bfloat16).reshape(groups * capacity, model_width).astype(jnp.float32)
    picked = summed[place].reshape(token_count, top_count, model_width)
    mixed = jnp.einsum("tk,tkd->td", forward_gates[0], picked)
    layer_out = (tokens.astype(jnp.float32) + mixed).astype(jnp.bfloat16)
    next_input = passed_along(layer_out, "segment", 1)
    return next_input[None]


def solution(mesh):
    in_specs = (
        P("segment", "expert", None),
        P("segment", "expert", None),
        P("segment", "expert", None),
        P("segment", "expert", None, None),
        P("segment", "expert", None, None),
        P("segment", "expert", None, None),
    )
    out_specs = P("segment", "expert", None)
    return jax.shard_map(local, mesh=mesh, in_specs=in_specs, out_specs=out_specs, check_vma=False)
```

profile of v0, /device:TPU:1, one launch (start us, length us, event | category | flops | bytes accessed | tf_op | source)
XLA Modules:
  0.0 403.4 jit_solution(7068611100493675159)
XLA Ops:
  0.0 0.0 copy-start
  0.0 0.0 copy-start.1
  0.0 0.8 eq.15
  0.8 0.7 broadcast_multiply_fusion
  1.5 0.1 fusion.31
  1.6 0.1 reduce_window_sum.11
  1.7 0.2 select_reduce_fusion
  1.8 0.1 mul.28
  2.0 0.8 scatter_custom_fusion.1
  2.8 0.8 scatter_custom_fusion
  3.6 0.1 broadcast_in_dim.34
  3.7 0.0 copy-done.1
  3.7 1.7 gather_fusion
  5.4 0.2 bitcast_select_fusion
  5.6 0.9 broadcast_in_dim.38
  6.5 0.0 copy-start.3
  6.5 178.2 %all_to_all.10 = bf16[64,8,7168]{2,1,0:T(8,128)(2,1)S(1)} all-to-all(bf16[64,8,7168]{2,1,0:T(8,128)(2,1)S(1)} %bitcast.57), channel_id=1, replica_groups=mesh['segment'=4,'expert'=64] {'expert'}, dimensions={0} | all-to-all | bytes 14680064 | tf_op jit(solution)/shard_map/all_to_all | solution.py:63
  184.7 0.0 copy-start.2
  184.7 3.0 copy-done.2
  187.7 0.0 copy-done.3
  187.7 2.1 fusion.3
  189.8 16.0 %fusion = bf16[64,8,7168]{2,1,0:T(8,128)(2,1)} fusion(bf16[1,1,256,7168]{3,2,1,0:T(8,128)(2,1)} %param.11, bf16[1,1,7168,256]{3,2,1,0:T(8,128)(2,1)} %param.10, bf16[64,8,7168]{2,1,0:T(8,128)(2,1)} %copy-done.2, f32[512,256]{1,0:T(8,128)S(1)} %fusion.3), kind=kOutput, calls=%fused_computation.5 | convolution fusion | flops 3762552832 | bytes 22544384 | tf_op jit(solution)/shard_map/dot_general | solution.py:37
  205.8 9.5 %all-to-all-start.1 = ((bf16[64,8,7168]{2,1,0:T(8,128)(2,1)}), bf16[64,8,7168]{2,1,0:T(8,128)(2,1)}, u32[]{:S(2)}, u32[]{:S(2)}) async-start(bf16[64,8,7168]{2,1,0:T(8,128)(2,1)} %fusion), calls=%async_computation.1 | async-start | bytes 14680064 | tf_op jit(solution)/shard_map/all_to_all | solution.py:65
  215.4 91.3 %all-to-all-done.1 = bf16[64,8,7168]{2,1,0:T(8,128)(2,1)} async-done(((bf16[64,8,7168]{2,1,0:T(8,128)(2,1)}), bf16[64,8,7168]{2,1,0:T(8,128)(2,1)}, u32[]{:S(2)}, u32[]{:S(2)}) %all-to-all-start.1) | async-done | bytes 7340064 | tf_op jit(solution)/shard_map/all_to_all | solution.py:65
  306.7 4.6 %reduce = bf16[16,8,7168]{2,1,0:T(8,128)(2,1)S(1)} reduce(bf16[4,16,8,7168]{3,2,1,0:T(8,128)(2,1)} %bitcast.10, bf16[]{:T(256)} %constant.34.clone.1), dimensions={0}, to_apply=%region_4.5.clone | reduce | flops 2752512 | bytes 9175042 | tf_op jit(solution)/shard_map/reduce_sum | solution.py:72
  311.2 1.1 gather_fusion.1
  312.4 0.0 copy-done
  312.4 0.4 fusion.18
  312.8 57.9 %collective-permute-start = (bf16[8,7168]{1,0:T(8,128)(2,1)S(1)}, bf16[8,7168]{1,0:T(8,128)(2,1)S(1)}, u32[]{:S(2)}, u32[]{:S(2)}) collective-permute-start(bf16[8,7168]{1,0:T(8,128)(2,1)S(1)} %fusion.30), channel_id=1, source_target_pairs={{0,64},{64,128},{128,192},{192,0},{1,65},{65,129},{129,193},{193,1... | collective-permute-start | bytes 344072 | tf_op jit(solution)/shard_map/ppermute | solution.py:12
  370.8 31.9 %collective-permute-done = bf16[8,7168]{1,0:T(8,128)(2,1)S(1)} collective-permute-done((bf16[8,7168]{1,0:T(8,128)(2,1)S(1)}, bf16[8,7168]{1,0:T(8,128)(2,1)S(1)}, u32[]{:S(2)}, u32[]{:S(2)}) %collective-permute-start) | collective-permute-done | bytes 114720 | tf_op jit(solution)/shard_map/ppermute | solution.py:12
  402.7 0.6 copy.11
  (8 shorter events, 0.1 us)
Async XLA Ops:
  0.0 312.4 %copy-start = (f32[1,8,8]{2,1,0:T(8,128)S(1)}, f32[1,8,8]{2,1,0:T(8,128)}, u32[]{:S(2)}) copy-start(f32[1,8,8]{2,1,0:T(8,128)} %param.8) | copy-start | bytes 772
  0.0 3.7 copy-start.1
  6.5 181.3 %copy-start.3 = (bf16[1,1,7168,256]{3,2,1,0:T(8,128)(2,1)S(1)}, bf16[1,1,7168,256]{3,2,1,0:T(8,128)(2,1)}, u32[]{:S(2)}) copy-start(bf16[1,1,7168,256]{3,2,1,0:T(8,128)(2,1)} %param.9) | copy-start | bytes 11010052
  184.7 3.0 copy-start.2
  205.8 100.9 %all-to-all-start.1 = ((bf16[64,8,7168]{2,1,0:T(8,128)(2,1)}), bf16[64,8,7168]{2,1,0:T(8,128)(2,1)}, u32[]{:S(2)}, u32[]{:S(2)}) async-start(bf16[64,8,7168]{2,1,0:T(8,128)(2,1)} %fusion), calls=%async_computation.1 | async-start | bytes 14680064 | tf_op jit(solution)/shard_map/all_to_all | solution.py:65
  312.8 89.9 %collective-permute-start = (bf16[8,7168]{1,0:T(8,128)(2,1)S(1)}, bf16[8,7168]{1,0:T(8,128)(2,1)S(1)}, u32[]{:S(2)}, u32[]{:S(2)}) collective-permute-start(bf16[8,7168]{1,0:T(8,128)(2,1)S(1)} %fusion.30), channel_id=1, source_target_pairs={{0,64},{64,128},{128,192},{192,0},{1,65},{65,129},{129,193},{193,1... | collective-permute-start | bytes 344072 | tf_op jit(solution)/shard_map/ppermute | solution.py:12
where the time goes:
time: 404 us; the launch traced here: 403 us
  blocking collectives  178 us (44%)
  waiting for transfers between devices  123 us (30%)
  starting transfers between devices  67.5 us (17%)
  matrix products  18.4 us (5%)
  local copies, waits for them, and re-layouts  9.91 us (2%)
  other arithmetic  5.87 us (1%)
    all_to_all x1, blocking collectives, local(): lax.all_to_all(copies, 'expert', split_axis=0, concat_axis=0, tiled=True)  178 us
    all_to_all x1, waiting for transfers between devices, local(): lax.all_to_all(result.reshape(devices, capacity, model_width), 'expert',...  91.3 us
    ppermute x1, starting transfers between devices, passed_along(): return lax.ppermute(value, axis, pairs)  57.9 us
    ppermute x1, waiting for transfers between devices, passed_along(): return lax.ppermute(value, axis, pairs)  31.9 us
    dot_general x1, matrix products, expert_forward(): jnp.dot(hidden, down_mat, preferred_element_type=jnp.float32)  16 us
    all_to_all x1, starting transfers between devices, local(): lax.all_to_all(result.reshape(devices, capacity, model_width), 'expert',...  9.55 us
  transfers between devices with their start and end apart: 2, of which 2 were waited for; matrix products, arithmetic and copies ran while one was open for 0% of the time, Pallas kernels for 0%

commit v1 on v0

v1 whole, which is shorter than its diff:
```python
import jax
import jax.numpy as jnp
from jax import lax
from jax.sharding import PartitionSpec as P

FH = 1024


def passed_along(value, axis, steps):
    count = lax.axis_size(axis)
    pairs = [(source, (source + steps) % count) for source in range(count)]
    return lax.ppermute(value, axis, pairs)


def local(forward_input, forward_routes, forward_gates, gate_matrix, up_matrix, down_matrix):
    devices = lax.axis_size("expert")
    hidden_slice = gate_matrix.shape[3]
    split = FH // hidden_slice
    groups = devices // split
    tokens = forward_input[0]
    me = lax.axis_index("expert")
    expert = me % groups
    rows = lax.all_gather(tokens, "expert", axis=0, tiled=True)
    routes = lax.all_gather(forward_routes[0], "expert", axis=0, tiled=True)
    gates = lax.all_gather(forward_gates[0], "expert", axis=0, tiled=True)
    weight = jnp.sum(jnp.where(routes == expert, gates, 0.0), axis=1)
    gate_act = jnp.dot(rows, gate_matrix[0, 0], preferred_element_type=jnp.float32)
    upper_act = jnp.dot(rows, up_matrix[0, 0], preferred_element_type=jnp.float32)
    hidden = (jax.nn.silu(gate_act) * upper_act).astype(jnp.bfloat16)
    partial = jnp.dot(hidden, down_matrix[0, 0], preferred_element_type=jnp.float32)
    partial = partial.astype(jnp.bfloat16).astype(jnp.float32)
    weighted = (weight[:, None] * partial).astype(jnp.bfloat16)
    mixed = lax.psum_scatter(weighted, "expert", scatter_dimension=0, tiled=True)
    layer_out = (tokens.astype(jnp.float32) + mixed.astype(jnp.float32)).astype(jnp.bfloat16)
    next_input = passed_along(layer_out, "segment", 1)
    return next_input[None]


def solution(mesh):
    in_specs = (
        P("segment", "expert", None),
        P("segment", "expert", None),
        P("segment", "expert", None),
        P("segment", "expert", None, None),
        P("segment", "expert", None, None),
        P("segment", "expert", None, None),
    )
    out_specs = P("segment", "expert", None)
    return jax.shard_map(local, mesh=mesh, in_specs=in_specs, out_specs=out_specs, check_vma=False)
```

time: 404 us -> 718 us (1.78); the launches traced: 403 us -> 710 us
  waiting for transfers between devices: 123 us -> 435 us
  starting transfers between devices: 67.5 us -> 0.12 us
  blocking collectives: 178 us -> 238 us
  between operations: 0.17 us -> 13.4 us
  local copies, waits for them, and re-layouts: 9.91 us -> 0.65 us
    reduce_scatter x0 -> x1, waiting for transfers between devices: none -> 428 us  [local(): lax.psum_scatter(weighted, 'expert', scatter_dimension=0, tiled=True)]
    all_gather x0 -> x2, blocking collectives: none -> 238 us  [the longest x1 129 us: local(): routes = lax.all_gather(forward_routes[0], 'expert', axis=0, tiled=True)]
    all_to_all x1 -> x0, blocking collectives: 178 us -> none  [local(): lax.all_to_all(copies, 'expert', split_axis=0, concat_axis=0, tiled=True)]
    all_to_all x1 -> x0, waiting for transfers between devices: 91.3 us -> none  [local(): lax.all_to_all(result.reshape(devices, capacity, model_width), 'expert',...]
    ppermute x1, starting transfers between devices: 57.9 us -> 0.08 us  [passed_along(): return lax.ppermute(value, axis, pairs)]
    ppermute x1, waiting for transfers between devices: 31.9 us -> 5.83 us  [passed_along(): return lax.ppermute(value, axis, pairs)]
    all_to_all x1 -> x0, starting transfers between devices: 9.55 us -> none  [local(): lax.all_to_all(result.reshape(devices, capacity, model_width), 'expert',...]
    dot_general x3 -> x2, matrix products: 18.4 us -> 22.1 us  [the longest x1 15.9 us: local(): jnp.dot(hidden, down_matrix[0, 0], preferred_element_type=jnp.float32)]
  transfers between devices with their start and end apart: 2 -> 3, of which waited for: 2 -> 2; matrix products, arithmetic and copies ran while one was open for 0% -> 0% of each run, Pallas kernels for 0% -> 0%
where the time goes in v1:
time: 718 us; the launch traced here: 710 us
  waiting for transfers between devices  435 us (61%)
  blocking collectives  238 us (33%)
  matrix products  22.1 us (3%)
  between operations  13.4 us (2%)
    reduce_scatter x1, waiting for transfers between devices, local(): lax.psum_scatter(weighted, 'expert', scatter_dimension=0, tiled=True)  428 us
    all_gather x1, blocking collectives, local(): routes = lax.all_gather(forward_routes[0], 'expert', axis=0, tiled=True)  129 us
    all_gather x1, blocking collectives, local(): gates = lax.all_gather(forward_gates[0], 'expert', axis=0, tiled=True)  109 us
    dot_general x1, matrix products, local(): jnp.dot(hidden, down_matrix[0, 0], preferred_element_type=jnp.float32)  15.9 us
  transfers between devices with their start and end apart: 3, of which 2 were waited for; matrix products, arithmetic and copies ran while one was open for 0% of the time, Pallas kernels for 0%

profile of v1, /device:TPU:1, one launch (start us, length us, event | category | flops | bytes accessed | tf_op | source)
XLA Modules:
  0.0 709.9 jit_solution(15679720350931443463)
XLA Ops:
  6.5 0.0 all-gather.5.cloned.1.call-start
  6.5 0.7 all-gather.5.cloned.1.call-update
  7.3 0.0 reduce-scatter.2.cloned.1.call-start
  7.3 128.8 %all-gather = s32[1,512,8]{2,1,0:T(8,128)S(1)} all-gather(s32[1,8,8]{2,1,0:T(8,128)} %param.7), channel_id=2, replica_groups=mesh['segment'=4,'expert'=64] {'expert'}, dimensions={1}, use_global_device_ids=true | all-gather | bytes 16640 | tf_op jit(solution)/shard_map/all_gather | solution.py:24
  136.1 109.0 %all-gather.1 = f32[1,512,8]{2,1,0:T(8,128)S(1)} all-gather(f32[1,8,8]{2,1,0:T(8,128)} %param.8), channel_id=3, replica_groups=mesh['segment'=4,'expert'=64] {'expert'}, dimensions={1}, use_global_device_ids=true | all-gather | bytes 16640 | tf_op jit(solution)/shard_map/all_gather | solution.py:25
  245.1 0.1 select_reduce_fusion
  245.2 0.0 all-gather.5.cloned.1.call-done
  245.3 6.2 fusion.2
  251.5 15.9 %multiply_convert_fusion = bf16[512,7168]{1,0:T(8,128)(2,1)} fusion(f32[512]{0:T(512)S(1)} %select_reduce_fusion, bf16[1,1,256,7168]{3,2,1,0:T(8,128)(2,1)} %param.11, bf16[1,1,7168,256]{3,2,1,0:T(8,128)(2,1)} %param.10, bf16[1,512,7168]{2,1,0:T(8,128)(2,1)} %all-gather.5.cloned.1.call-done, f32[512,256]{1,0:T(8,128)S(1)} %fusion.2), kind=kOutput, calls=%fused_computation | convolution fusion | flops 3773562880 | bytes 22546432 | tf_op jit(solution)/shard_map/dot_general | solution.py:30
  267.4 0.0 copy-start
  267.4 0.0 reduce-scatter.2.cloned.1.call-update
  267.4 428.2 %reduce-scatter.2.cloned.1.call-done = bf16[8,7168]{1,0:T(8,128)(2,1)} async-done(((bf16[512,7168]{1,0:T(8,128)(2,1)}), bf16[8,7168]{1,0:T(8,128)(2,1)}) %reduce-scatter.2.cloned.1.call-update) | async-done | bytes 114704 | tf_op jit(solution)/shard_map/reduce_scatter | solution.py:33
  695.6 0.0 copy-done
  695.6 0.9 fusion.17
  696.5 0.1 collective-permute-start
  696.6 5.8 collective-permute-done
  702.4 0.6 copy.8
Async XLA Ops:
  6.5 238.7 %all-gather.5.cloned.1.call-start = ((), (), s32[]{:S(2)}) async-start(), calls=%async_computation.2 | async-start | bytes 7454720 | tf_op jit(solution)/shard_map/all_gather | solution.py:23
  7.3 688.3 %reduce-scatter.2.cloned.1.call-start = ((), (), s32[]{:S(2)}) async-start(), calls=%async_computation.1 | async-start | bytes 7454720 | tf_op jit(solution)/shard_map/reduce_scatter | solution.py:33
  267.4 428.2 %copy-start = (bf16[1,8,7168]{2,1,0:T(8,128)(2,1)S(1)}, bf16[1,8,7168]{2,1,0:T(8,128)(2,1)}, u32[]{:S(2)}) copy-start(bf16[1,8,7168]{2,1,0:T(8,128)(2,1)} %param.6) | copy-start | bytes 344068
  696.5 5.9 collective-permute-start
Sparse Core Ops, SparseCore 0:
  10.8 113.3 all-gather.4
  267.6 427.9 reduce-scatter.1
